TPU v7x, 256 devices: a whole 4x4x8 slice. The times are simulated.
256 devices in a mesh: dp: 16 (over z, core), seq: 16 (over y, x).
Axes of the slice: x: 4, y: 4, z: 8, core: 2. Of those that a mesh axis runs over, the one named last changes fastest.
Arguments:
- clean_frames: bfloat16 [16, 2048, 1024], P('dp', 'seq')
- noise_frames: bfloat16 [16, 2048, 1024], P('dp', 'seq'), may hold values from -6 to 6
- lengths: int32 [16], P('dp'), may hold values from 512 to 2048
- group_ids: int32 [16, 2048], P('dp'), may hold values from 0 to 255, never falling along the last dimension, each value on 1 to 25 neighbouring positions
- time_index: int32 [16], P('dp'), may hold values from 0 to 999
- modulation: float32 [1024], replicated, may hold values from -4 to 4
- teacher_qkv: bfloat16 [1024, 3072], replicated, may hold values from -0.1875 to 0.1875
- teacher_out: bfloat16 [1024, 1024], replicated, may hold values from -6 to 6
- student_in: bfloat16 [3, 1024, 1024], P(None, ('dp', 'seq')), may hold values from -0.1875 to 0.1875
- student_out: bfloat16 [1024, 1024], P(('dp', 'seq')), may hold values from -1 to 1
Outputs:
- grad_inputs: float32 [2, 1024, 1024], P(None, ('dp', 'seq'))
- mean_error: float32 [], replicated
Inputs may be any that keep to these rules, and one draw needn't show every extreme that they name: `group_ids`: group numbers never fall along a dialogue, and each group holds 1 to 25 frames.
All inputs are finite; a program needn't handle non-finite values.
Results may differ from a plain program's by a relative error of at most 0.015.
Values may be sent and summed in bfloat16 or wider, within the bound.
No kernel may reach another device: no remote copies, remote signals or barrier semaphores. Data moves between devices by JAX's collectives and lax.ppermute only.
A program may use at most 128 MiB of HBM per device.

v0:
```python
import jax
import jax.numpy as jnp
from jax import lax
from jax.sharding import PartitionSpec as P

HEADS = 16
HALO = 64
TSTEPS = 1000
EPSILON = 1e-06
NEGATIVE = -1e30


def with_halo(block, sides, width):
    for axis, dim in sides:
        count = lax.axis_size(axis)
        forward = [(i, i + 1) for i in range(count - 1)]
        backward = [(target, source) for source, target in forward]
        low = lax.ppermute(
            lax.slice_in_dim(block, block.shape[dim] - width, None, axis=dim), axis, forward
        )
        high = lax.ppermute(lax.slice_in_dim(block, 0, width, axis=dim), axis, backward)
        block = jnp.concatenate([low, block, high], axis=dim)
    return block


def from_behind(block, axis, distance):
    devices = range(lax.axis_size(axis))
    route = [(i - distance, i) for i in devices if i - distance in devices]
    return lax.ppermute(block, axis, route)


def normalize(clean_frames, noise_frames, time_index, modulation):
    flow_time = (time_index.astype(jnp.float32) + 0.5) / TSTEPS
    flow_time = flow_time[:, None, None]
    blended = (1.0 - flow_time) * noise_frames.astype(
        jnp.float32
    ) + flow_time * clean_frames.astype(jnp.float32)
    inv_rms = lax.rsqrt(jnp.mean(blended * blended, axis=-1, keepdims=True) + EPSILON)
    return (blended * inv_rms * (1.0 + flow_time * modulation)).astype(jnp.bfloat16)


def attend_block(queries, key_rows, values, key_bias):
    scores = jnp.dot(queries, key_rows.T, preferred_element_type=jnp.float32) * queries.shape[
        -1
    ] ** (-0.5)
    scores = scores + key_bias[None, :]
    row_max = jnp.max(scores, axis=-1, keepdims=True)
    exponent = jnp.exp(scores - row_max)
    probs_low = (exponent / jnp.sum(exponent, axis=-1, keepdims=True)).astype(jnp.bfloat16)
    return jnp.dot(probs_low, values, preferred_element_type=jnp.float32).astype(jnp.bfloat16)


def full_attention(queries, key_rows, values, key_bias):
    total_rows = queries.shape[0]
    block_rows = min(512, total_rows)
    blocked = queries.reshape(total_rows // block_rows, block_rows, queries.shape[1])
    result = lax.map(lambda piece: attend_block(piece, key_rows, values, key_bias), blocked)
    return result.reshape(total_rows, values.shape[1])


def teacher_heads(proj_one, bias_one):
    stacked = jnp.transpose(proj_one, (2, 1, 0, 3))
    result = lax.map(
        lambda element: full_attention(element[0], element[1], element[2], bias_one), stacked
    )
    return jnp.transpose(result, (1, 0, 2))


def build_allowed(query_group, query_pos, key_group, key_pos, lengths):
    same_group = key_group[:, None, :] == query_group[:, :, None]
    prev_group = key_group[:, None, :] == query_group[:, :, None] - 1
    live_key = (key_pos[None, :] < lengths[:, None]) & (key_pos[None, :] >= 0)
    itself = key_pos[None, :] == query_pos[:, None]
    return (same_group | prev_group) & (live_key[:, None, :] | itself[None])


def split_product(form, gradient, other, first):
    upper_part = gradient.astype(jnp.bfloat16)
    lower_part = (gradient - upper_part.astype(jnp.float32)).astype(jnp.bfloat16)
    if first:
        return jnp.einsum(form, upper_part, other, preferred_element_type=jnp.float32) + jnp.einsum(
            form, lower_part, other, preferred_element_type=jnp.float32
        )
    return jnp.einsum(form, other, upper_part, preferred_element_type=jnp.float32) + jnp.einsum(
        form, other, lower_part, preferred_element_type=jnp.float32
    )


def total_of(value):
    spread = jnp.broadcast_to(value, (lax.axis_size("seq"), 128))
    spread = lax.all_to_all(spread, "seq", 0, 0, tiled=True).sum(0, keepdims=True)
    spread = jnp.broadcast_to(spread, (lax.axis_size("dp"), 128))
    spread = lax.all_to_all(spread, "dp", 0, 0, tiled=True).sum(0)
    return spread[0]


def shards(
    clean_frames,
    noise_frames,
    lengths,
    group_ids,
    time_index,
    modulation,
    teacher_qkv,
    teacher_out,
    student_in,
    student_out,
):
    dialogs, shard_rows, model_width = clean_frames.shape
    head_dim = model_width // HEADS
    seq_count = lax.axis_size("seq")
    seq_index = lax.axis_index("seq")
    frames = shard_rows * seq_count
    window = shard_rows + 2 * HALO
    rows_each = student_out.shape[0]
    stacked = jnp.concatenate((student_in.reshape(3 * rows_each, model_width), student_out), axis=0)
    gathered = lax.all_gather(lax.all_gather(stacked, "seq", axis=0), "dp", axis=0)
    gathered = gathered.reshape(-1, 4 * rows_each, model_width)
    w_inputs = (
        gathered[:, : 3 * rows_each]
        .reshape(-1, 3, rows_each, model_width)
        .transpose(1, 0, 2, 3)
        .reshape(3, -1, model_width)
    )
    w_output = gathered[:, 3 * rows_each :].reshape(-1, model_width)
    frame_count = jnp.sum(lax.all_gather(lengths, "dp", axis=0, tiled=True)).astype(jnp.float32)
    normed = normalize(clean_frames, noise_frames, time_index, modulation)
    flat_rows = normed.reshape(dialogs * shard_rows, model_width)
    frame_pos = jnp.arange(frames, dtype=jnp.int32)
    key_bias = jnp.where(frame_pos[None, :] < lengths[:, None], 0.0, NEGATIVE).astype(jnp.float32)
    teacher_proj = jnp.dot(flat_rows, teacher_qkv, preferred_element_type=jnp.float32).astype(
        jnp.bfloat16
    )
    teacher_proj = teacher_proj.reshape(dialogs, shard_rows, 3, HEADS, head_dim)
    by_heads = lax.all_to_all(teacher_proj, "seq", split_axis=3, concat_axis=1, tiled=True)
    head_out = lax.map(lambda element: teacher_heads(element[0], element[1]), (by_heads, key_bias))
    by_frames = lax.all_to_all(head_out, "seq", split_axis=1, concat_axis=2, tiled=True)
    teacher_vel = jnp.dot(
        by_frames.reshape(dialogs * shard_rows, model_width),
        teacher_out,
        preferred_element_type=jnp.float32,
    )
    offset = seq_index * shard_rows
    queries = jnp.dot(flat_rows, w_inputs[0], preferred_element_type=jnp.float32).astype(
        jnp.bfloat16
    )
    queries = queries.reshape(dialogs, shard_rows, HEADS, head_dim)
    key_local = jnp.dot(flat_rows, w_inputs[1], preferred_element_type=jnp.float32).astype(
        jnp.bfloat16
    )
    value_local = jnp.dot(flat_rows, w_inputs[2], preferred_element_type=jnp.float32).astype(
        jnp.bfloat16
    )
    both_local = jnp.concatenate((key_local, value_local), axis=-1).reshape(
        dialogs, shard_rows, 2 * model_width
    )
    both_window = with_halo(both_local, (("seq", 1),), HALO)
    key_rows = both_window[:, :, :model_width].reshape(dialogs, window, HEADS, head_dim)
    value_rows = both_window[:, :, model_width:].reshape(dialogs, window, HEADS, head_dim)
    group_pad = jnp.pad(group_ids, ((0, 0), (HALO, HALO)), constant_values=-10)
    key_group = lax.dynamic_slice_in_dim(group_pad, offset, window, 1)
    query_group = lax.dynamic_slice_in_dim(group_ids, offset, shard_rows, 1)
    query_pos = offset + jnp.arange(shard_rows, dtype=jnp.int32)
    key_pos = offset - HALO + jnp.arange(window, dtype=jnp.int32)
    allowed = build_allowed(query_group, query_pos, key_group, key_pos, lengths)
    scaling = head_dim ** (-0.5)
    scores = jnp.einsum("brhd,bwhd->bhrw", queries, key_rows, preferred_element_type=jnp.float32)
    scores = jnp.where(allowed[:, None], scores * scaling, NEGATIVE)
    row_max = jnp.max(scores, axis=-1, keepdims=True)
    exponent = jnp.exp(scores - row_max)
    probs = exponent / jnp.sum(exponent, axis=-1, keepdims=True)
    probs_low = probs.astype(jnp.bfloat16)
    student_mix = jnp.einsum(
        "bhrw,bwhd->brhd", probs_low, value_rows, preferred_element_type=jnp.float32
    ).astype(jnp.bfloat16)
    mix_flat = student_mix.reshape(dialogs * shard_rows, model_width)
    student_vel = jnp.dot(mix_flat, w_output, preferred_element_type=jnp.float32)
    query_valid = (query_pos[None, :] < lengths[:, None]).reshape(-1)
    difference = jnp.where(query_valid[:, None], student_vel - teacher_vel, 0.0)
    square_sum = total_of(jnp.sum(difference * difference))
    mean_error = square_sum / (frame_count * model_width)
    grad_vel = (difference * lax.rsqrt(frame_count)).astype(jnp.bfloat16)
    grad_mix = jnp.dot(grad_vel, w_output.T, preferred_element_type=jnp.float32).astype(
        jnp.bfloat16
    )
    grad_mix = grad_mix.reshape(dialogs, shard_rows, HEADS, head_dim)
    grad_prob = jnp.einsum(
        "brhd,bwhd->bhrw", grad_mix, value_rows, preferred_element_type=jnp.float32
    )
    grad_score = probs * (grad_prob - jnp.sum(probs * grad_prob, axis=-1, keepdims=True)) * scaling
    grad_key = split_product("bhrw,brhd->bwhd", grad_score, queries, True)
    grad_value = jnp.einsum(
        "bhrw,brhd->bwhd", probs_low, grad_mix, preferred_element_type=jnp.float32
    )
    grad_both = jnp.concatenate(
        (
            grad_key.reshape(dialogs, window, model_width),
            grad_value.reshape(dialogs, window, model_width),
        ),
        axis=-1,
    )
    from_next = from_behind(grad_both[:, :HALO].astype(jnp.bfloat16), "seq", -1).astype(jnp.float32)
    from_prev = from_behind(
        grad_both[:, HALO + shard_rows :].astype(jnp.bfloat16), "seq", 1
    ).astype(jnp.float32)
    owned_rows = grad_both[:, HALO : HALO + shard_rows]
    owned_rows = owned_rows.at[:, :HALO].add(from_prev)
    owned_rows = owned_rows.at[:, shard_rows - HALO :].add(from_next)
    by_head = owned_rows.reshape(shard_rows, 2, HEADS, head_dim).transpose(0, 2, 1, 3)
    head_grads = lax.all_to_all(by_head, "seq", split_axis=1, concat_axis=0, tiled=True)
    head_grads = head_grads.reshape(frames, 2 * head_dim)
    normed_all = lax.all_gather(flat_rows, "seq", axis=0, tiled=True)
    partial = split_product("rf,rg->fg", head_grads, normed_all, False)
    dp_count = lax.axis_size("dp")
    partial = partial.reshape(dp_count, seq_count, rows_each, 2 * head_dim)
    partial = lax.all_to_all(partial, "dp", split_axis=0, concat_axis=0, tiled=True).sum(0)
    mine = lax.all_to_all(partial, "seq", split_axis=0, concat_axis=0, tiled=True)
    mine = mine.reshape(HEADS, rows_each, 2, head_dim).transpose(2, 1, 0, 3)
    grad_inputs = mine.reshape(2, rows_each, model_width)
    return (grad_inputs, mean_error)


def solution(mesh):
    in_specs = (
        P("dp", "seq", None),
        P("dp", "seq", None),
        P("dp"),
        P("dp", None),
        P("dp"),
        P(),
        P(),
        P(),
        P(None, ("dp", "seq"), None),
        P(("dp", "seq"), None),
    )
    out_specs = (P(None, ("dp", "seq"), None), P())
    return jax.shard_map(shards, mesh=mesh, in_specs=in_specs, out_specs=out_specs, check_vma=False)
```

profile of v0, /device:TPU:1, one launch (start us, length us, event | category | flops | bytes accessed | tf_op | source)
XLA Modules:
  0.0 354.5 jit_solution(4930259637896913242)
XLA Ops:
  8.8 21.8 %all-gather.1 = bf16[256,1024]{1,0:T(8,128)(2,1)} all-gather(bf16[16,1024]{1,0:T(8,128)(2,1)S(1)} %pad_maximum_fusion.2), channel_id=3, replica_groups=mesh['dp'=16,'seq'=16] {'seq'}, dimensions={0}, use_global_device_ids=true | all-gather | bytes 557056 | tf_op jit(solution)/shard_map/all_gather | solution.py:117
  34.4 3.9 %convolution_convert_fusion = bf16[128,3072]{1,0:T(8,128)(2,1)S(1)} fusion(bf16[1024,3072]{1,0:T(8,128)(2,1)} %param.22, bf16[1,128,1024]{2,1,0:T(8,128)(2,1)S(1)} %multiply_convert_fusion.1), kind=kOutput, calls=%fused_computation.23 | convolution fusion | flops 805699584 | bytes 7340032 | tf_op jit(solution)/shard_map/dot_general | solution.py:131
  39.5 2.1 copy.97
  41.6 4.7 %all-to-all-start = ((bf16[1,128,3,16,64]{1,4,2,0,3:T(8,128)(2,1)}), bf16[1,128,3,16,64]{1,4,2,0,3:T(8,128)(2,1)S(1)}, u32[]{:S(2)}, u32[]{:S(2)}) async-start(bf16[1,128,3,16,64]{1,4,2,0,3:T(8,128)(2,1)} %copy.97), calls=%async_computation | async-start | bytes 1572864 | tf_op jit(solution)/shard_map/all_to_all | solution.py:135
  47.9 8.9 %all-to-all-done = bf16[1,128,3,16,64]{1,4,2,0,3:T(8,128)(2,1)S(1)} async-done(((bf16[1,128,3,16,64]{1,4,2,0,3:T(8,128)(2,1)}), bf16[1,128,3,16,64]{1,4,2,0,3:T(8,128)(2,1)S(1)}, u32[]{:S(2)}, u32[]{:S(2)}) %all-to-all-start) | async-done | bytes 786464 | tf_op jit(solution)/shard_map/all_to_all | solution.py:135
  64.1 17.6 %while.29 = (s32[]{:T(128)}, bf16[4,512,64]{1,2,0:T(8,128)(2,1)}, bf16[4,512,64]{2,1,0:T(8,128)(2,1)S(1)}, bf16[2048,64]{1,0:T(8,128)(2,1)S(1)}, bf16[2048,64]{1,0:T(8,128)(2,1)}, /*index=5*/s32[]{:T(128)}, s32[]{:T(128)}) while((s32[]{:T(128)}, bf16[4,512,64]{1,2,0:T(8,128)(2,1)}, bf16[4,512,64]{2,1,0:T(8,128)(2,1)S(1)}, ...), condition=%wide.region_6.7_spmd.clone, body=%wide.region_3.6_spmd.clone.sunk | while | flops 281054208 | bytes 14658161 | solution.py:57
  71.0 1.9 fusion.101
  75.4 1.9 fusion.101
  79.8 1.9 fusion.101
  81.7 2.0 copy.114
  83.7 3.3 reshape.458
  87.5 12.4 %reduce.14 = bf16[2048,64]{1,0:T(8,128)(2,1)} reduce(bf16[2048,1,1,64]{3,2,1,0:T(2,128)(2,1)S(1)} %bitcast.156, bf16[]{:T(256)} %broadcast.275), dimensions={1,2}, to_apply=%bitcast.107.reduce_sub_computation | reduce | bytes 524290
  99.9 2.2 reshape.459
  102.0 3.5 all-to-all-start.1
  106.9 21.3 %all-reduce.1 = s32[16]{0:T(128)S(1)} all-reduce(s32[16]{0:T(128)S(1)} %dynamic-update-slice.6), channel_id=1, replica_groups=mesh['dp'=16,'seq'=16] {'dp'}, use_global_device_ids=true, to_apply=%add.1 | all-reduce | flops 16 | bytes 128
  131.1 7.2 %copy.116 = bf16[256,12,1024]{2,0,1:T(8,128)(2,1)S(1)} copy(bf16[256,12,1024]{2,1,0:T(8,128)(2,1)} %bitcast.144) | data formatting | bytes 12582912
  138.3 3.4 fusion.64
  141.6 2.9 copy.93
  144.6 4.0 %squeeze.45 = bf16[1024,1024]{1,0:T(8,128)(2,1)} reshape(bf16[1,256,4,1024]{3,2,1,0:T(4,128)(2,1)} %copy.93) | data formatting | bytes 4194304 | tf_op jit(solution)/shard_map/squeeze | solution.py:151
  148.5 4.5 %copy.92 = bf16[1,256,4,1024]{3,2,1,0:T(4,128)(2,1)} copy(bf16[1,256,4,1024]{3,1,2,0:T(8,128)(2,1)} %get-tuple-element.142) | data formatting | bytes 4194304 | tf_op jit(solution)/shard_map/slice | solution.py:148
  153.1 4.0 %squeeze.44 = bf16[1024,1024]{1,0:T(8,128)(2,1)} reshape(bf16[1,256,4,1024]{3,2,1,0:T(4,128)(2,1)} %copy.92) | data formatting | bytes 4194304 | tf_op jit(solution)/shard_map/squeeze | solution.py:148
  157.1 2.2 convolution_convert_fusion.3
  160.7 4.0 %collective-permute-start = (bf16[1,64,2048]{2,1,0:T(8,128)(2,1)}, bf16[1,64,2048]{2,1,0:T(8,128)(2,1)}, u32[]{:S(2)}, u32[]{:S(2)}) collective-permute-start(bf16[1,64,2048]{2,1,0:T(8,128)(2,1)} %get-tuple-element.152), channel_id=1, source_target_pairs={{0,1},{1,2},{2,3},{3,4},{4,5},{5,6},{6,7},{7,8},{8,9},{9,10},{10,1... | collective-permute-start | bytes 786440 | tf_op jit(solution)/shard_map/ppermute | solution.py:18
  166.0 3.0 copy.90
  168.9 4.2 %squeeze.43 = bf16[1024,1024]{1,0:T(8,128)(2,1)} reshape(bf16[1,256,4,1024]{3,2,1,0:T(4,128)(2,1)} %copy.90) | data formatting | bytes 4194304 | tf_op jit(solution)/shard_map/squeeze | solution.py:144
  173.1 2.0 convolution_convert_fusion.5
  176.0 4.6 %slice.137 = bf16[256,4,1024]{2,1,0:T(4,128)(2,1)} slice(bf16[256,16,1024]{2,1,0:T(8,128)(2,1)} %all-gather.8.cloned.1.call-done), slice={[0:256], [12:16], [0:1024]} | slice | bytes 4194304 | tf_op jit(solution)/shard_map/slice | solution.py:125
  180.6 4.0 %reshape.438 = bf16[1024,1024]{1,0:T(8,128)(2,1)} reshape(bf16[256,4,1024]{2,1,0:T(4,128)(2,1)} %slice.137) | data formatting | bytes 4194304 | tf_op jit(solution)/shard_map/reshape | solution.py:125
  187.0 3.2 fusion.68
  190.2 2.3 convolution_convert_fusion.2
  197.0 15.6 %fusion.38 = f32[16,64,256]{2,1,0:T(8,128)} fusion(bf16[128,16,64]{0,2,1:T(8,128)(2,1)S(1)} %bitcast.173, f32[16,128,256]{2,1,0:T(8,128)} %fusion.70, f32[16,128,256]{2,1,0:T(8,128)} %get-tuple-element.155, f32[16,128]{1,0:T(8,128)S(1)} %get-tuple-element.154), kind=kOutput, calls=%fused_computation.61 | convolution fusion | flops 70781184 | bytes 5513216 | tf_op jit(solution)/shard_map/bhrw,brhd->bwhd/dot_general | solution.py:81
  212.6 14.9 %convolution_add_fusion = f32[16,64,256]{2,1,0:T(8,128)S(1)} fusion(f32[16,64,256]{2,1,0:T(8,128)} %fusion.38, bf16[128,16,64]{0,2,1:T(8,128)(2,1)} %bitcast.172, f32[16,128,256]{2,1,0:T(8,128)} %fusion.70, f32[16,128,256]{2,1,0:T(8,128)} %get-tuple-element.155, f32[16,128]{1,0:T(8,128)S(1)} %get-tuple-element.154), kind=kOutput, calls=%fused_computation.37 | convolution fusion | flops 72616192 | bytes 6561792 | tf_op jit(solution)/shard_map/bhrw,brhd->bwhd/dot_general | solution.py:81
  227.6 2.1 fusion.48
  230.9 4.0 %collective-permute-start.2 = (bf16[1,64,2048]{1,2,0:T(8,128)(2,1)S(1)}, bf16[1,64,2048]{1,2,0:T(8,128)(2,1)S(1)}, u32[]{:S(2)}, u32[]{:S(2)}) collective-permute-start(bf16[1,64,2048]{1,2,0:T(8,128)(2,1)S(1)} %get-tuple-element.146), channel_id=1, source_target_pairs={{0,1},{1,2},{2,3},{3,4},{4,5},{5,6},{6,7},{7,8},{8,9},{9,10},{10,1... | collective-permute-start | bytes 786440 | tf_op jit(solution)/shard_map/ppermute | solution.py:29
  237.5 5.9 %collective-permute-done.2 = bf16[1,64,2048]{1,2,0:T(8,128)(2,1)S(1)} collective-permute-done((bf16[1,64,2048]{1,2,0:T(8,128)(2,1)S(1)}, bf16[1,64,2048]{1,2,0:T(8,128)(2,1)S(1)}, u32[]{:S(2)}, u32[]{:S(2)}) %collective-permute-start.2) | collective-permute-done | bytes 262176 | tf_op jit(solution)/shard_map/ppermute | solution.py:29
  244.7 5.7 %scatter-add.6 = f32[1,128,2048]{1,2,0:T(8,128)} dynamic-update-slice(f32[1,128,2048]{1,2,0:T(8,128)} %fusion.29, f32[1,64,2048]{1,2,0:T(8,128)} %fusion.31, s32[]{:T(128)} %constant.131.clone.1, s32[]{:T(128)} %constant.131.clone.1, s32[]{:T(128)} %constant.131.clone.1) | dynamic-update-slice | bytes 1048580 | tf_op jit(solution)/shard_map/scatter-add | solution.py:207
  250.4 2.8 slice_add_fusion
  253.2 8.6 %scatter-add.9 = f32[1,128,2048]{1,2,0:T(8,128)S(1)} dynamic-update-slice(f32[1,128,2048]{1,2,0:T(8,128)S(1)} %copy-done.5, f32[1,64,2048]{1,2,0:T(8,128)} %slice_add_fusion, s32[]{:T(128)} %constant.131.clone.1, s32[]{:T(128)} %constant.142.clone.1, s32[]{:T(128)} %constant.131.clone.1) | dynamic-update-slice | bytes 1048580 | tf_op jit(solution)/shard_map/scatter-add | solution.py:208
  262.0 21.2 %all_to_all.67 = f32[128,16,2,64]{0,3,2,1:T(8,128)} all-to-all(f32[128,16,2,64]{0,3,2,1:T(8,128)S(1)} %copy.107), channel_id=1, replica_groups=mesh['dp'=16,'seq'=16] {'seq'}, dimensions={1} | all-to-all | bytes 2097152 | tf_op jit(solution)/shard_map/all_to_all | solution.py:210
  284.5 3.5 all-to-all-start.5
  289.8 3.7 %fusion.16 = f32[1024,128]{1,0:T(8,128)S(1)} fusion(bf16[1,2048,1024]{2,1,0:T(8,128)(2,1)} %all-gather.6.cloned.1.call-done, f32[16,8,16,128]{3,2,1,0:T(8,128)S(1)} %bitcast.152), kind=kOutput, calls=%fused_computation.19 | convolution fusion | flops 537919488 | bytes 5767168 | tf_op jit(solution)/shard_map/rf,rg->fg/dot_general | solution.py:84
  293.5 2.3 fusion.25
  295.8 8.3 %all-to-all-start.3 = ((f32[16,16,4,128]{3,2,1,0:T(4,128)}), f32[16,16,4,128]{3,2,1,0:T(4,128)S(1)}, u32[]{:S(2)}, u32[]{:S(2)}) async-start(f32[16,16,4,128]{3,2,1,0:T(4,128)} %bitcast.164), calls=%async_computation.3 | async-start | bytes 1048576 | tf_op jit(solution)/shard_map/all_to_all | solution.py:216
  304.2 17.3 %all-to-all-done.3 = f32[16,16,4,128]{3,2,1,0:T(4,128)S(1)} async-done(((f32[16,16,4,128]{3,2,1,0:T(4,128)}), f32[16,16,4,128]{3,2,1,0:T(4,128)S(1)}, u32[]{:S(2)}, u32[]{:S(2)}) %all-to-all-start.3) | async-done | bytes 524320 | tf_op jit(solution)/shard_map/all_to_all | solution.py:216
  322.1 3.3 all-to-all-start.6
  326.1 5.9 %all-to-all-done.6 = f32[16,1,128]{2,1,0:T(1,128)S(1)} async-done(((f32[16,1,128]{2,1,0:T(1,128)}), f32[16,1,128]{2,1,0:T(1,128)S(1)}, u32[]{:S(2)}, u32[]{:S(2)}) %all-to-all-start.6) | async-done | bytes 8224 | tf_op jit(solution)/shard_map/all_to_all | solution.py:93
  332.1 6.9 %all-to-all-start.4 = ((f32[16,4,128]{2,1,0:T(4,128)}), f32[16,4,128]{2,1,0:T(4,128)S(1)}, u32[]{:S(2)}, u32[]{:S(2)}) async-start(f32[16,4,128]{2,1,0:T(4,128)} %reduce_sum.85), calls=%async_computation.4 | async-start | bytes 65536 | tf_op jit(solution)/shard_map/all_to_all | solution.py:217
  339.0 6.4 %all-to-all-done.4 = f32[16,4,128]{2,1,0:T(4,128)S(1)} async-done(((f32[16,4,128]{2,1,0:T(4,128)}), f32[16,4,128]{2,1,0:T(4,128)S(1)}, u32[]{:S(2)}, u32[]{:S(2)}) %all-to-all-start.4) | async-done | bytes 32800 | tf_op jit(solution)/shard_map/all_to_all | solution.py:217
  (113 shorter events, 50.7 us)
Async XLA Ops:
  7.2 185.8 %copy-start = (bf16[1024,1024]{1,0:T(8,128)(2,1)S(1)}, bf16[1024,1024]{1,0:T(8,128)(2,1)}, u32[]{:S(2)}) copy-start(bf16[1024,1024]{1,0:T(8,128)(2,1)} %param.23) | copy-start | bytes 6291460
  7.2 123.9 %all-gather.8.cloned.1.call-start = ((), (), s32[]{:S(2)}) async-start(), calls=%async_computation.8 | async-start | bytes 8912896 | tf_op jit(solution)/shard_map/all_gather | solution.py:117
  34.4 3.9 %copy-start.3 = (bf16[1,128,1024]{2,1,0:T(8,128)(2,1)}, bf16[1,128,1024]{2,1,0:T(8,128)(2,1)S(1)}, u32[]{:S(2)}) copy-start(bf16[1,128,1024]{2,1,0:T(8,128)(2,1)S(1)} %multiply_convert_fusion.1) | copy-start | bytes 786436
  39.5 8.3 %copy-start.10 = (s32[1,2048]{1,0:T(1,128)S(1)}, s32[1,2048]{1,0:T(1,128)}, u32[]{:S(2)}) copy-start(s32[1,2048]{1,0:T(1,128)} %param.19) | copy-start | bytes 24580
  41.6 15.2 %all-to-all-start = ((bf16[1,128,3,16,64]{1,4,2,0,3:T(8,128)(2,1)}), bf16[1,128,3,16,64]{1,4,2,0,3:T(8,128)(2,1)S(1)}, u32[]{:S(2)}, u32[]{:S(2)}) async-start(bf16[1,128,3,16,64]{1,4,2,0,3:T(8,128)(2,1)} %copy.97), calls=%async_computation | async-start | bytes 1572864 | tf_op jit(solution)/shard_map/all_to_all | solution.py:135
  46.4 243.4 %all-gather.6.cloned.1.call-start = ((), (), s32[]{:S(2)}) async-start(), calls=%async_computation.7 | async-start | bytes 4456448 | tf_op jit(solution)/shard_map/all_gather | solution.py:212
  65.6 1.0 copy-start.8
  70.0 1.0 copy-start.8
  74.3 1.1 copy-start.8
  78.7 1.1 copy-start.8
  83.7 21.9 %copy-start.11 = (u32[256]{0:T(256)S(1)}, u32[256]{0:T(256)}, u32[]{:S(2)}) copy-start(u32[256]{0:T(256)} %constant.155) | copy-start | bytes 3076
  102.0 27.6 %all-to-all-start.1 = ((bf16[16,2,4096]{2,1,0:T(2,128)(2,1)}), bf16[16,2,4096]{2,1,0:T(2,128)(2,1)S(1)}, u32[]{:S(2)}, u32[]{:S(2)}) async-start(bf16[16,2,4096]{2,1,0:T(2,128)(2,1)} %reshape.459), calls=%async_computation.1 | async-start | bytes 524288 | tf_op jit(solution)/shard_map/all_to_all | solution.py:137
  153.1 4.0 %copy-start.4 = (bf16[1,128,1024]{2,1,0:T(8,128)(2,1)S(1)}, bf16[1,128,1024]{2,1,0:T(8,128)(2,1)}, u32[]{:S(2)}) copy-start(bf16[1,128,1024]{2,1,0:T(8,128)(2,1)} %copy-done.3) | copy-start | bytes 786436
  157.1 2.2 copy-start.6
  159.3 6.6 %copy-start.7 = (bf16[1,256,4,1024]{3,1,2,0:T(8,128)(2,1)S(1)}, bf16[1,256,4,1024]{3,1,2,0:T(8,128)(2,1)}, u32[]{:S(2)}) copy-start(bf16[1,256,4,1024]{3,1,2,0:T(8,128)(2,1)} %get-tuple-element.144) | copy-start | bytes 6291460
  160.7 23.9 %collective-permute-start = (bf16[1,64,2048]{2,1,0:T(8,128)(2,1)}, bf16[1,64,2048]{2,1,0:T(8,128)(2,1)}, u32[]{:S(2)}, u32[]{:S(2)}) collective-permute-start(bf16[1,64,2048]{2,1,0:T(8,128)(2,1)} %get-tuple-element.152), channel_id=1, source_target_pairs={{0,1},{1,2},{2,3},{3,4},{4,5},{5,6},{6,7},{7,8},{8,9},{9,10},{10,1... | collective-permute-start | bytes 786440 | tf_op jit(solution)/shard_map/ppermute | solution.py:18
  164.7 19.9 %collective-permute-start.1 = (bf16[1,64,2048]{2,1,0:T(8,128)(2,1)}, bf16[1,64,2048]{2,1,0:T(8,128)(2,1)}, u32[]{:S(2)}, u32[]{:S(2)}) collective-permute-start(bf16[1,64,2048]{2,1,0:T(8,128)(2,1)} %get-tuple-element.153), channel_id=1, source_target_pairs={{1,0},{2,1},{3,2},{4,3},{5,4},{6,5},{7,6},{8,7},{9,8},{10,9},{11,1... | collective-permute-start | bytes 786440 | tf_op jit(solution)/shard_map/ppermute | solution.py:21
  190.2 2.3 copy-start.2
  194.9 2.0 copy-start.9
  230.9 12.5 %collective-permute-start.2 = (bf16[1,64,2048]{1,2,0:T(8,128)(2,1)S(1)}, bf16[1,64,2048]{1,2,0:T(8,128)(2,1)S(1)}, u32[]{:S(2)}, u32[]{:S(2)}) collective-permute-start(bf16[1,64,2048]{1,2,0:T(8,128)(2,1)S(1)} %get-tuple-element.146), channel_id=1, source_target_pairs={{0,1},{1,2},{2,3},{3,4},{4,5},{5,6},{6,7},{7,8},{8,9},{9,10},{10,1... | collective-permute-start | bytes 786440 | tf_op jit(solution)/shard_map/ppermute | solution.py:29
  234.9 15.6 %collective-permute-start.3 = (bf16[1,64,2048]{1,2,0:T(8,128)(2,1)}, bf16[1,64,2048]{1,2,0:T(8,128)(2,1)}, u32[]{:S(2)}, u32[]{:S(2)}) collective-permute-start(bf16[1,64,2048]{1,2,0:T(8,128)(2,1)} %get-tuple-element.145), channel_id=1, source_target_pairs={{1,0},{2,1},{3,2},{4,3},{5,4},{6,5},{7,6},{8,7},{9,8},{10,9},{11,1... | collective-permute-start | bytes 786440 | tf_op jit(solution)/shard_map/ppermute | solution.py:29
  250.4 2.8 copy-start.5
  284.5 11.3 %all-to-all-start.5 = ((f32[16,1,128]{2,1,0:T(1,128)}), f32[16,1,128]{2,1,0:T(1,128)S(1)}, u32[]{:S(2)}, u32[]{:S(2)}) async-start(f32[16,1,128]{2,1,0:T(1,128)} %broadcast_in_dim.59), calls=%async_computation.5 | async-start | bytes 16384 | tf_op jit(solution)/shard_map/all_to_all | solution.py:91
  289.8 3.7 %copy-start.1 = (bf16[1,2048,1024]{2,1,0:T(8,128)(2,1)S(1)}, bf16[1,2048,1024]{2,1,0:T(8,128)(2,1)}, u32[]{:S(2)}) copy-start(bf16[1,2048,1024]{2,1,0:T(8,128)(2,1)} %all-gather.6.cloned.1.call-done) | copy-start | bytes 12582916
  295.8 25.7 %all-to-all-start.3 = ((f32[16,16,4,128]{3,2,1,0:T(4,128)}), f32[16,16,4,128]{3,2,1,0:T(4,128)S(1)}, u32[]{:S(2)}, u32[]{:S(2)}) async-start(f32[16,16,4,128]{3,2,1,0:T(4,128)} %bitcast.164), calls=%async_computation.3 | async-start | bytes 1048576 | tf_op jit(solution)/shard_map/all_to_all | solution.py:216
  322.1 10.0 %all-to-all-start.6 = ((f32[16,1,128]{2,1,0:T(1,128)}), f32[16,1,128]{2,1,0:T(1,128)S(1)}, u32[]{:S(2)}, u32[]{:S(2)}) async-start(f32[16,1,128]{2,1,0:T(1,128)} %broadcast_in_dim.88), calls=%async_computation.6 | async-start | bytes 16384 | tf_op jit(solution)/shard_map/all_to_all | solution.py:93
  332.1 13.3 %all-to-all-start.4 = ((f32[16,4,128]{2,1,0:T(4,128)}), f32[16,4,128]{2,1,0:T(4,128)S(1)}, u32[]{:S(2)}, u32[]{:S(2)}) async-start(f32[16,4,128]{2,1,0:T(4,128)} %reduce_sum.85), calls=%async_computation.4 | async-start | bytes 65536 | tf_op jit(solution)/shard_map/all_to_all | solution.py:217
Sparse Core Ops, SparseCore 0:
  30.7 62.3 all-gather.7
  95.6 56.0 all-gather.5
where the time goes:
time: 359 us; the launch traced here: 354 us
  local copies, waits for them, and re-layouts  87.6 us (24%)
  matrix products  67.7 us (19%)
  blocking collectives  64.3 us (18%)
  waiting for transfers between devices  44.6 us (12%)
  starting transfers between devices  41.5 us (12%)
  other arithmetic  30.8 us (9%)
  between operations  18 us (5%)
    all_gather x1, blocking collectives, shards(): lax.all_gather(stacked, 'seq', axis=0)  21.8 us
    unnamed x1, blocking collectives  21.3 us
    all_to_all x1, blocking collectives, shards(): lax.all_to_all(by_head, 'seq', split_axis=1, concat_axis=0, tiled=True)  21.2 us
    all_to_all x1, waiting for transfers between devices, shards(): lax.all_to_all(partial, 'dp', split_axis=0, concat_axis=0, tiled=True)  17.3 us
    dot_general x1, matrix products, split_product(): jnp.einsum(form, upper_part, other, preferred_element_type=jnp.float32)  15.6 us
    unnamed x33, local copies, waits for them, and re-layouts  15.5 us
    dot_general x1, matrix products, split_product(): jnp.einsum(form, lower_part, other, preferred_element_type=jnp.float32)  14.9 us
    unnamed x1, other arithmetic  12.4 us
  transfers between devices with their start and end apart: 12, of which 5 were waited for; matrix products, arithmetic and copies ran while one was open for 51% of the time, Pallas kernels for 0%

commit v1 on v0

--- a/solution.py
+++ b/solution.py
@@ -1,3 +1,4 @@
+import functools
 import jax
 import jax.numpy as jnp
 from jax import lax
@@ -8,6 +9,18 @@
 TSTEPS = 1000
 EPSILON = 1e-06
 NEGATIVE = -1e30
+
+
+def launch_the_sizes(here_x, which_dim, dimension_no):
+    part_next = jax.lax.axis_size("seq")
+    everything = jnp.split(here_x, part_next, which_dim)
+    z2 = jnp.stack(everything)
+    o_now = jax.lax.all_to_all(z2, axis_name="seq", split_axis=0, concat_axis=0)
+    y1 = jnp.concatenate(o_now, dimension_no)
+    return y1
+
+
+cover_series_up = functools.partial(launch_the_sizes, which_dim=3, dimension_no=1)
 
 
 def with_halo(block, sides, width):
@@ -132,7 +145,7 @@
         jnp.bfloat16
     )
     teacher_proj = teacher_proj.reshape(dialogs, shard_rows, 3, HEADS, head_dim)
-    by_heads = lax.all_to_all(teacher_proj, "seq", split_axis=3, concat_axis=1, tiled=True)
+    by_heads = cover_series_up(teacher_proj)
     head_out = lax.map(lambda element: teacher_heads(element[0], element[1]), (by_heads, key_bias))
     by_frames = lax.all_to_all(head_out, "seq", split_axis=1, concat_axis=2, tiled=True)
     teacher_vel = jnp.dot(

time: 359 us -> 381 us (1.061)
  local copies, waits for them, and re-layouts: 87.6 us -> 107 us
    unnamed x33 -> x48, local copies, waits for them, and re-layouts: 15.5 us -> 35.4 us
  transfers between devices with their start and end apart: 12 -> 12, of which waited for: 5 -> 5; matrix products, arithmetic and copies ran while one was open for 51% -> 54% of each run, Pallas kernels for 0% -> 0%
where the time goes in v1:
time: 381 us; the launch traced here: 375 us
  local copies, waits for them, and re-layouts  107 us (28%)
  matrix products  67.7 us (18%)
  blocking collectives  65.1 us (17%)
  waiting for transfers between devices  44.3 us (12%)
  starting transfers between devices  41.9 us (11%)
  other arithmetic  30.8 us (8%)
  between operations  18 us (5%)
    unnamed x48, local copies, waits for them, and re-layouts  35.4 us
    all_to_all x1, blocking collectives, shards(): lax.all_to_all(by_head, 'seq', split_axis=1, concat_axis=0, tiled=True)  22 us
    all_gather x1, blocking collectives, shards(): lax.all_gather(stacked, 'seq', axis=0)  21.8 us
    unnamed x1, blocking collectives  21.4 us
    all_to_all x1, waiting for transfers between devices, shards(): lax.all_to_all(partial, 'dp', split_axis=0, concat_axis=0, tiled=True)  17.3 us
    dot_general x1, matrix products, split_product(): jnp.einsum(form, upper_part, other, preferred_element_type=jnp.float32)  15.6 us
    dot_general x1, matrix products, split_product(): jnp.einsum(form, lower_part, other, preferred_element_type=jnp.float32)  14.9 us
    unnamed x1, other arithmetic  12.4 us
  transfers between devices with their start and end apart: 12, of which 5 were waited for; matrix products, arithmetic and copies ran while one was open for 54% of the time, Pallas kernels for 0%

profile of v1, /device:TPU:1, one launch (start us, length us, event | category | flops | bytes accessed | tf_op | source)
XLA Modules:
  0.0 375.2 jit_solution(11478219585746661527)
XLA Ops:
  8.8 21.8 %all-gather.1 = bf16[256,1024]{1,0:T(8,128)(2,1)} all-gather(bf16[16,1024]{1,0:T(8,128)(2,1)S(1)} %pad_maximum_fusion.2), channel_id=3, replica_groups=mesh['dp'=16,'seq'=16] {'seq'}, dimensions={0}, use_global_device_ids=true | all-gather | bytes 557056 | tf_op jit(solution)/shard_map/all_gather | solution.py:130
  34.4 3.9 %convolution_convert_fusion = bf16[128,3072]{1,0:T(8,128)(2,1)S(1)} fusion(bf16[1024,3072]{1,0:T(8,128)(2,1)} %param.22, bf16[1,128,1024]{2,1,0:T(8,128)(2,1)S(1)} %multiply_convert_fusion.1), kind=kOutput, calls=%fused_computation.23 | convolution fusion | flops 805699584 | bytes 7340032 | tf_op jit(solution)/shard_map/dot_general | solution.py:144
  62.2 4.8 %all-to-all-start = ((bf16[16,1,128,3,1,64]{2,5,3,4,1,0:T(8,128)(2,1)}), bf16[16,1,128,3,1,64]{2,5,3,4,1,0:T(8,128)(2,1)S(1)}, u32[]{:S(2)}, u32[]{:S(2)}) async-start(bf16[16,1,128,3,1,64]{2,5,3,4,1,0:T(8,128)(2,1)} %fusion.58), calls=%async_computation | async-start | bytes 1572864 | tf_op jit(solution)/shard_map/all_to_all | solution.py:18
  68.5 8.9 %all-to-all-done = bf16[16,1,128,3,1,64]{2,5,3,4,1,0:T(8,128)(2,1)S(1)} async-done(((bf16[16,1,128,3,1,64]{2,5,3,4,1,0:T(8,128)(2,1)}), bf16[16,1,128,3,1,64]{2,5,3,4,1,0:T(8,128)(2,1)S(1)}, u32[]{:S(2)}, u32[]{:S(2)}) %all-to-all-start) | async-done | bytes 786464 | tf_op jit(solution)/shard_map/all_to_all | solution.py:18
  81.1 2.0 copy.188
  83.6 17.6 %while.29 = (s32[]{:T(128)}, bf16[4,512,64]{1,2,0:T(8,128)(2,1)}, bf16[4,512,64]{2,1,0:T(8,128)(2,1)S(1)}, bf16[2048,64]{1,0:T(8,128)(2,1)S(1)}, bf16[2048,64]{1,0:T(8,128)(2,1)}, /*index=5*/s32[]{:T(128)}, s32[]{:T(128)}) while((s32[]{:T(128)}, bf16[4,512,64]{1,2,0:T(8,128)(2,1)}, bf16[4,512,64]{2,1,0:T(8,128)(2,1)S(1)}, ...), condition=%wide.region_6.7_spmd.clone, body=%wide.region_3.6_spmd.clone.sunk | while | flops 281054208 | bytes 14657661 | solution.py:70
  90.5 1.9 fusion.117
  94.9 1.9 fusion.117
  99.3 1.9 fusion.117
  101.2 2.0 copy.201
  103.2 3.3 reshape.459
  107.0 12.4 %reduce.14 = bf16[2048,64]{1,0:T(8,128)(2,1)} reduce(bf16[2048,1,1,64]{3,2,1,0:T(2,128)(2,1)S(1)} %bitcast.247, bf16[]{:T(256)} %broadcast.275), dimensions={1,2}, to_apply=%bitcast.198.reduce_sub_computation | reduce | bytes 524290
  119.3 2.2 reshape.460
  121.5 3.5 all-to-all-start.1
  126.4 21.4 %all-reduce.1 = s32[16]{0:T(128)S(1)} all-reduce(s32[16]{0:T(128)S(1)} %dynamic-update-slice.6), channel_id=1, replica_groups=mesh['dp'=16,'seq'=16] {'dp'}, use_global_device_ids=true, to_apply=%add.1 | all-reduce | flops 16 | bytes 128
  150.7 6.9 %copy.203 = bf16[256,12,1024]{2,0,1:T(8,128)(2,1)S(1)} copy(bf16[256,12,1024]{2,1,0:T(8,128)(2,1)} %bitcast.235) | data formatting | bytes 12582912
  157.6 3.0 fusion.80
  160.5 4.6 %slice.137 = bf16[256,4,1024]{2,1,0:T(4,128)(2,1)} slice(bf16[256,16,1024]{2,1,0:T(8,128)(2,1)} %all-gather.8.cloned.1.call-done), slice={[0:256], [12:16], [0:1024]} | slice | bytes 4194304 | tf_op jit(solution)/shard_map/slice | solution.py:138
  165.1 4.0 %reshape.439 = bf16[1024,1024]{1,0:T(8,128)(2,1)} reshape(bf16[256,4,1024]{2,1,0:T(4,128)(2,1)} %slice.137) | data formatting | bytes 4194304 | tf_op jit(solution)/shard_map/reshape | solution.py:138
  169.1 4.5 %copy.165 = bf16[1,256,4,1024]{3,2,1,0:T(4,128)(2,1)} copy(bf16[1,256,4,1024]{3,1,2,0:T(8,128)(2,1)} %get-tuple-element.142) | data formatting | bytes 4194304 | tf_op jit(solution)/shard_map/slice | solution.py:161
  173.6 3.9 %squeeze.44 = bf16[1024,1024]{1,0:T(8,128)(2,1)} reshape(bf16[1,256,4,1024]{3,2,1,0:T(4,128)(2,1)} %copy.165) | data formatting | bytes 4194304 | tf_op jit(solution)/shard_map/squeeze | solution.py:161
  177.6 4.5 %copy.166 = bf16[1,256,4,1024]{3,2,1,0:T(4,128)(2,1)} copy(bf16[1,256,4,1024]{3,1,2,0:T(8,128)(2,1)} %get-tuple-element.143) | data formatting | bytes 4194304 | tf_op jit(solution)/shard_map/slice | solution.py:164
  182.1 4.0 %squeeze.45 = bf16[1024,1024]{1,0:T(8,128)(2,1)} reshape(bf16[1,256,4,1024]{3,2,1,0:T(4,128)(2,1)} %copy.166) | data formatting | bytes 4194304 | tf_op jit(solution)/shard_map/squeeze | solution.py:164
  186.1 2.2 convolution_convert_fusion.4
  189.7 4.1 %collective-permute-start = (bf16[1,64,2048]{2,1,0:T(8,128)(2,1)}, bf16[1,64,2048]{2,1,0:T(8,128)(2,1)}, u32[]{:S(2)}, u32[]{:S(2)}) collective-permute-start(bf16[1,64,2048]{2,1,0:T(8,128)(2,1)} %get-tuple-element.152), channel_id=1, source_target_pairs={{0,1},{1,2},{2,3},{3,4},{4,5},{5,6},{6,7},{7,8},{8,9},{9,10},{10,1... | collective-permute-start | bytes 786440 | tf_op jit(solution)/shard_map/ppermute | solution.py:31
  195.3 2.9 copy.163
  198.3 4.0 %squeeze.43 = bf16[1024,1024]{1,0:T(8,128)(2,1)} reshape(bf16[1,256,4,1024]{3,2,1,0:T(4,128)(2,1)} %copy.163) | data formatting | bytes 4194304 | tf_op jit(solution)/shard_map/squeeze | solution.py:157
  202.2 2.0 convolution_convert_fusion.5
  207.5 3.2 fusion.84
  210.7 2.3 convolution_convert_fusion.2
  217.5 15.6 %fusion.38 = f32[16,64,256]{2,1,0:T(8,128)} fusion(bf16[128,16,64]{0,2,1:T(8,128)(2,1)S(1)} %bitcast.278, f32[16,128,256]{2,1,0:T(8,128)} %fusion.86, f32[16,128,256]{2,1,0:T(8,128)} %get-tuple-element.155, f32[16,128]{1,0:T(8,128)S(1)} %get-tuple-element.154), kind=kOutput, calls=%fused_computation.61 | convolution fusion | flops 70781184 | bytes 5513216 | tf_op jit(solution)/shard_map/bhrw,brhd->bwhd/dot_general | solution.py:94
  233.1 14.9 %convolution_add_fusion = f32[16,64,256]{2,1,0:T(8,128)S(1)} fusion(f32[16,64,256]{2,1,0:T(8,128)} %fusion.38, bf16[128,16,64]{0,2,1:T(8,128)(2,1)} %bitcast.277, f32[16,128,256]{2,1,0:T(8,128)} %fusion.86, f32[16,128,256]{2,1,0:T(8,128)} %get-tuple-element.155, f32[16,128]{1,0:T(8,128)S(1)} %get-tuple-element.154), kind=kOutput, calls=%fused_computation.37 | convolution fusion | flops 72616192 | bytes 6561792 | tf_op jit(solution)/shard_map/bhrw,brhd->bwhd/dot_general | solution.py:94
  248.1 2.1 fusion.48
  251.4 4.0 %collective-permute-start.2 = (bf16[1,64,2048]{1,2,0:T(8,128)(2,1)S(1)}, bf16[1,64,2048]{1,2,0:T(8,128)(2,1)S(1)}, u32[]{:S(2)}, u32[]{:S(2)}) collective-permute-start(bf16[1,64,2048]{1,2,0:T(8,128)(2,1)S(1)} %get-tuple-element.146), channel_id=1, source_target_pairs={{0,1},{1,2},{2,3},{3,4},{4,5},{5,6},{6,7},{7,8},{8,9},{9,10},{10,1... | collective-permute-start | bytes 786440 | tf_op jit(solution)/shard_map/ppermute | solution.py:42
  258.2 5.5 %collective-permute-done.2 = bf16[1,64,2048]{1,2,0:T(8,128)(2,1)S(1)} collective-permute-done((bf16[1,64,2048]{1,2,0:T(8,128)(2,1)S(1)}, bf16[1,64,2048]{1,2,0:T(8,128)(2,1)S(1)}, u32[]{:S(2)}, u32[]{:S(2)}) %collective-permute-start.2) | collective-permute-done | bytes 262176 | tf_op jit(solution)/shard_map/ppermute | solution.py:42
  265.1 5.4 %scatter-add.6 = f32[1,128,2048]{1,2,0:T(8,128)} dynamic-update-slice(f32[1,128,2048]{1,2,0:T(8,128)} %fusion.29, f32[1,64,2048]{1,2,0:T(8,128)} %fusion.31, s32[]{:T(128)} %constant.131.clone.1, s32[]{:T(128)} %constant.131.clone.1, s32[]{:T(128)} %constant.131.clone.1) | dynamic-update-slice | bytes 1048580 | tf_op jit(solution)/shard_map/scatter-add | solution.py:220
  270.6 2.8 slice_add_fusion
  273.4 8.6 %scatter-add.9 = f32[1,128,2048]{1,2,0:T(8,128)S(1)} dynamic-update-slice(f32[1,128,2048]{1,2,0:T(8,128)S(1)} %copy-done.5, f32[1,64,2048]{1,2,0:T(8,128)} %slice_add_fusion, s32[]{:T(128)} %constant.131.clone.1, s32[]{:T(128)} %constant.142.clone.1, s32[]{:T(128)} %constant.131.clone.1) | dynamic-update-slice | bytes 1048580 | tf_op jit(solution)/shard_map/scatter-add | solution.py:221
  282.1 22.0 %all_to_all.57 = f32[128,16,2,64]{0,3,2,1:T(8,128)} all-to-all(f32[128,16,2,64]{0,3,2,1:T(8,128)S(1)} %copy.194), channel_id=1, replica_groups=mesh['dp'=16,'seq'=16] {'seq'}, dimensions={1} | all-to-all | bytes 2097152 | tf_op jit(solution)/shard_map/all_to_all | solution.py:223
  305.3 3.5 all-to-all-start.5
  310.7 3.7 fusion.16
  314.4 2.3 fusion.25
  316.7 8.2 %all-to-all-start.3 = ((f32[16,16,4,128]{3,2,1,0:T(4,128)}), f32[16,16,4,128]{3,2,1,0:T(4,128)S(1)}, u32[]{:S(2)}, u32[]{:S(2)}) async-start(f32[16,16,4,128]{3,2,1,0:T(4,128)} %bitcast.269), calls=%async_computation.3 | async-start | bytes 1048576 | tf_op jit(solution)/shard_map/all_to_all | solution.py:229
  324.9 17.3 %all-to-all-done.3 = f32[16,16,4,128]{3,2,1,0:T(4,128)S(1)} async-done(((f32[16,16,4,128]{3,2,1,0:T(4,128)}), f32[16,16,4,128]{3,2,1,0:T(4,128)S(1)}, u32[]{:S(2)}, u32[]{:S(2)}) %all-to-all-start.3) | async-done | bytes 524320 | tf_op jit(solution)/shard_map/all_to_all | solution.py:229
  342.8 3.3 all-to-all-start.6
  346.8 5.9 %all-to-all-done.6 = f32[16,1,128]{2,1,0:T(1,128)S(1)} async-done(((f32[16,1,128]{2,1,0:T(1,128)}), f32[16,1,128]{2,1,0:T(1,128)S(1)}, u32[]{:S(2)}, u32[]{:S(2)}) %all-to-all-start.6) | async-done | bytes 8224 | tf_op jit(solution)/shard_map/all_to_all | solution.py:106
  352.7 6.9 %all-to-all-start.4 = ((f32[16,4,128]{2,1,0:T(4,128)}), f32[16,4,128]{2,1,0:T(4,128)S(1)}, u32[]{:S(2)}, u32[]{:S(2)}) async-start(f32[16,4,128]{2,1,0:T(4,128)} %reduce_sum.85), calls=%async_computation.4 | async-start | bytes 65536 | tf_op jit(solution)/shard_map/all_to_all | solution.py:230
  359.7 6.4 %all-to-all-done.4 = f32[16,4,128]{2,1,0:T(4,128)S(1)} async-done(((f32[16,4,128]{2,1,0:T(4,128)}), f32[16,4,128]{2,1,0:T(4,128)S(1)}, u32[]{:S(2)}, u32[]{:S(2)}) %all-to-all-start.4) | async-done | bytes 32800 | tf_op jit(solution)/shard_map/all_to_all | solution.py:230
  (128 shorter events, 70.8 us)
Async XLA Ops:
  7.2 206.3 %copy-start = (bf16[1024,1024]{1,0:T(8,128)(2,1)S(1)}, bf16[1024,1024]{1,0:T(8,128)(2,1)}, u32[]{:S(2)}) copy-start(bf16[1024,1024]{1,0:T(8,128)(2,1)} %param.23) | copy-start | bytes 6291460
  7.2 143.5 %all-gather.8.cloned.1.call-start = ((), (), s32[]{:S(2)}) async-start(), calls=%async_computation.8 | async-start | bytes 8912896 | tf_op jit(solution)/shard_map/all_gather | solution.py:130
  34.4 3.9 %copy-start.3 = (bf16[1,128,1024]{2,1,0:T(8,128)(2,1)}, bf16[1,128,1024]{2,1,0:T(8,128)(2,1)S(1)}, u32[]{:S(2)}) copy-start(bf16[1,128,1024]{2,1,0:T(8,128)(2,1)S(1)} %multiply_convert_fusion.1) | copy-start | bytes 786436
  39.5 28.9 %copy-start.10 = (s32[1,2048]{1,0:T(1,128)S(1)}, s32[1,2048]{1,0:T(1,128)}, u32[]{:S(2)}) copy-start(s32[1,2048]{1,0:T(1,128)} %param.19) | copy-start | bytes 24580
  62.2 15.2 %all-to-all-start = ((bf16[16,1,128,3,1,64]{2,5,3,4,1,0:T(8,128)(2,1)}), bf16[16,1,128,3,1,64]{2,5,3,4,1,0:T(8,128)(2,1)S(1)}, u32[]{:S(2)}, u32[]{:S(2)}) async-start(bf16[16,1,128,3,1,64]{2,5,3,4,1,0:T(8,128)(2,1)} %fusion.58), calls=%async_computation | async-start | bytes 1572864 | tf_op jit(solution)/shard_map/all_to_all | solution.py:18
  67.0 243.7 %all-gather.6.cloned.1.call-start = ((), (), s32[]{:S(2)}) async-start(), calls=%async_computation.7 | async-start | bytes 4456448 | tf_op jit(solution)/shard_map/all_gather | solution.py:225
  85.1 1.0 copy-start.8
  89.5 1.0 copy-start.8
  93.9 1.0 copy-start.8
  98.2 1.0 copy-start.8
  103.2 21.9 %copy-start.11 = (u32[256]{0:T(256)S(1)}, u32[256]{0:T(256)}, u32[]{:S(2)}) copy-start(u32[256]{0:T(256)} %constant.155) | copy-start | bytes 3076
  121.5 27.8 %all-to-all-start.1 = ((bf16[16,2,4096]{2,1,0:T(2,128)(2,1)}), bf16[16,2,4096]{2,1,0:T(2,128)(2,1)S(1)}, u32[]{:S(2)}, u32[]{:S(2)}) async-start(bf16[16,2,4096]{2,1,0:T(2,128)(2,1)} %reshape.460), calls=%async_computation.1 | async-start | bytes 524288 | tf_op jit(solution)/shard_map/all_to_all | solution.py:150
  182.1 4.0 %copy-start.4 = (bf16[1,128,1024]{2,1,0:T(8,128)(2,1)S(1)}, bf16[1,128,1024]{2,1,0:T(8,128)(2,1)}, u32[]{:S(2)}) copy-start(bf16[1,128,1024]{2,1,0:T(8,128)(2,1)} %copy-done.3) | copy-start | bytes 786436
  186.1 2.2 copy-start.6
  188.3 7.0 %copy-start.7 = (bf16[1,256,4,1024]{3,1,2,0:T(8,128)(2,1)S(1)}, bf16[1,256,4,1024]{3,1,2,0:T(8,128)(2,1)}, u32[]{:S(2)}) copy-start(bf16[1,256,4,1024]{3,1,2,0:T(8,128)(2,1)} %get-tuple-element.144) | copy-start | bytes 6291460
  189.7 15.4 %collective-permute-start = (bf16[1,64,2048]{2,1,0:T(8,128)(2,1)}, bf16[1,64,2048]{2,1,0:T(8,128)(2,1)}, u32[]{:S(2)}, u32[]{:S(2)}) collective-permute-start(bf16[1,64,2048]{2,1,0:T(8,128)(2,1)} %get-tuple-element.152), channel_id=1, source_target_pairs={{0,1},{1,2},{2,3},{3,4},{4,5},{5,6},{6,7},{7,8},{8,9},{9,10},{10,1... | collective-permute-start | bytes 786440 | tf_op jit(solution)/shard_map/ppermute | solution.py:31
  193.8 11.3 %collective-permute-start.1 = (bf16[1,64,2048]{2,1,0:T(8,128)(2,1)}, bf16[1,64,2048]{2,1,0:T(8,128)(2,1)}, u32[]{:S(2)}, u32[]{:S(2)}) collective-permute-start(bf16[1,64,2048]{2,1,0:T(8,128)(2,1)} %get-tuple-element.153), channel_id=1, source_target_pairs={{1,0},{2,1},{3,2},{4,3},{5,4},{6,5},{7,6},{8,7},{9,8},{10,9},{11,1... | collective-permute-start | bytes 786440 | tf_op jit(solution)/shard_map/ppermute | solution.py:34
  210.7 2.3 copy-start.2
  215.5 2.0 copy-start.9
  251.4 12.4 %collective-permute-start.2 = (bf16[1,64,2048]{1,2,0:T(8,128)(2,1)S(1)}, bf16[1,64,2048]{1,2,0:T(8,128)(2,1)S(1)}, u32[]{:S(2)}, u32[]{:S(2)}) collective-permute-start(bf16[1,64,2048]{1,2,0:T(8,128)(2,1)S(1)} %get-tuple-element.146), channel_id=1, source_target_pairs={{0,1},{1,2},{2,3},{3,4},{4,5},{5,6},{6,7},{7,8},{8,9},{9,10},{10,1... | collective-permute-start | bytes 786440 | tf_op jit(solution)/shard_map/ppermute | solution.py:42
  255.4 15.2 %collective-permute-start.3 = (bf16[1,64,2048]{1,2,0:T(8,128)(2,1)}, bf16[1,64,2048]{1,2,0:T(8,128)(2,1)}, u32[]{:S(2)}, u32[]{:S(2)}) collective-permute-start(bf16[1,64,2048]{1,2,0:T(8,128)(2,1)} %get-tuple-element.145), channel_id=1, source_target_pairs={{1,0},{2,1},{3,2},{4,3},{5,4},{6,5},{7,6},{8,7},{9,8},{10,9},{11,1... | collective-permute-start | bytes 786440 | tf_op jit(solution)/shard_map/ppermute | solution.py:42
  270.6 2.8 copy-start.5
  305.3 11.4 %all-to-all-start.5 = ((f32[16,1,128]{2,1,0:T(1,128)}), f32[16,1,128]{2,1,0:T(1,128)S(1)}, u32[]{:S(2)}, u32[]{:S(2)}) async-start(f32[16,1,128]{2,1,0:T(1,128)} %broadcast_in_dim.59), calls=%async_computation.5 | async-start | bytes 16384 | tf_op jit(solution)/shard_map/all_to_all | solution.py:104
  310.7 3.7 copy-start.1
  316.7 25.5 %all-to-all-start.3 = ((f32[16,16,4,128]{3,2,1,0:T(4,128)}), f32[16,16,4,128]{3,2,1,0:T(4,128)S(1)}, u32[]{:S(2)}, u32[]{:S(2)}) async-start(f32[16,16,4,128]{3,2,1,0:T(4,128)} %bitcast.269), calls=%async_computation.3 | async-start | bytes 1048576 | tf_op jit(solution)/shard_map/all_to_all | solution.py:229
  342.8 10.0 %all-to-all-start.6 = ((f32[16,1,128]{2,1,0:T(1,128)}), f32[16,1,128]{2,1,0:T(1,128)S(1)}, u32[]{:S(2)}, u32[]{:S(2)}) async-start(f32[16,1,128]{2,1,0:T(1,128)} %broadcast_in_dim.88), calls=%async_computation.6 | async-start | bytes 16384 | tf_op jit(solution)/shard_map/all_to_all | solution.py:106
  352.7 13.3 %all-to-all-start.4 = ((f32[16,4,128]{2,1,0:T(4,128)}), f32[16,4,128]{2,1,0:T(4,128)S(1)}, u32[]{:S(2)}, u32[]{:S(2)}) async-start(f32[16,4,128]{2,1,0:T(4,128)} %reduce_sum.85), calls=%async_computation.4 | async-start | bytes 65536 | tf_op jit(solution)/shard_map/all_to_all | solution.py:230
Sparse Core Ops, SparseCore 0:
  30.7 62.3 all-gather.7
  95.6 55.8 all-gather.5
